TPU v7x, 32 devices: a whole 2x2x4 slice. The times are simulated.
32 devices in a mesh: bl: 4 (over y, x), freq: 8 (over z, core).
Axes of the slice: x: 2, y: 2, z: 4, core: 2. Of those that a mesh axis runs over, the one named last changes fastest.
Arguments:
- visibility: bfloat16 [2, 64, 1024, 4096], P(None, None, 'freq', 'bl'), may hold values from -6 to 6
- mode_index: int32 [256], replicated, may hold values from 0 to 2047
- beam_mode_weights: bfloat16 [256, 64, 64], replicated, may hold values from -0.75 to 0.75
- inverse_cov: float32 [256, 1024, 1024], P(('bl', 'freq')), may hold values from -2 to 3, as said below
- noise_power: float32 [256, 1024], P(('bl', 'freq')), may hold values from 0.2 to 2
Outputs:
- filtered: float32 [256, 1024, 128], P(('bl', 'freq'))
Inputs may be any that keep to these rules, and one draw needn't show every extreme that they name: Each inverse_cov[m] is symmetric positive definite.
All inputs are finite; a program needn't handle non-finite values.
Results may differ from a plain program's by a relative error of at most 0.0023.
Values may be sent and summed in bfloat16 or wider, within the bound.
No kernel may reach another device: no remote copies, remote signals or barrier semaphores. Data moves between devices by JAX's collectives and lax.ppermute only.
A program may use at most 192 MiB of HBM per device.

v0:
```python
import math
import jax
import jax.numpy as jnp
from jax import lax
from jax.sharding import PartitionSpec as P


def dft_table(mode_index, sample_ids, length):
    phase_steps = mode_index[None, :] * sample_ids[:, None] % length
    phases = phase_steps.astype(jnp.float32) * (2.0 * math.pi / length)
    norming = 1.0 / math.sqrt(length)
    cosine = jnp.cos(phases) * norming
    sine_part = jnp.sin(phases) * norming
    real_rows = jnp.concatenate([cosine, -sine_part], axis=1)
    imag_rows = jnp.concatenate([sine_part, cosine], axis=1)
    return jnp.stack([real_rows, imag_rows]).astype(jnp.bfloat16)


def transform(samples, dft_weights):
    return lax.dot_general(
        samples, dft_weights, (((0, 3), (0, 1)), ((), ())), preferred_element_type=jnp.float32
    )


def project(spectrum, beam_rows):
    row_count, freq_count, column_total = spectrum.shape
    mode_count = column_total // 2
    halves = spectrum.reshape(row_count, freq_count, 2, mode_count)
    projected = jnp.einsum(
        "bfcm,msb->mfcs", halves, beam_rows.astype(jnp.float32), precision=lax.Precision.HIGHEST
    )
    return projected.reshape(mode_count, freq_count, 2 * beam_rows.shape[1])


def weigh_all(inverse_cov, noise_power, owner_modes):
    weighted = jnp.einsum("mfg,mgk->mfk", inverse_cov, owner_modes, precision=lax.Precision.HIGHEST)
    return owner_modes - noise_power[:, :, None] * weighted


def body(visibility, mode_index, beam_mode_weights, inverse_cov, noise_power):
    bl_devices = lax.axis_size("bl")
    local_times = visibility.shape[3]
    total_times = local_times * bl_devices
    sample_ids = lax.axis_index("bl") * local_times + jnp.arange(local_times, dtype=jnp.int32)
    dft_weights = dft_table(mode_index, sample_ids, total_times)
    partial_terms = project(transform(visibility, dft_weights), beam_mode_weights)
    summed_modes = lax.psum_scatter(partial_terms, "bl", scatter_dimension=0, tiled=True)
    owner_modes = lax.all_to_all(summed_modes, "freq", split_axis=0, concat_axis=1, tiled=True)
    return weigh_all(inverse_cov, noise_power, owner_modes)


def solution(mesh):
    placed = (
        P(None, None, "freq", "bl"),
        P(),
        P(),
        P(("bl", "freq"), None, None),
        P(("bl", "freq"), None),
    )
    return jax.shard_map(
        body, mesh=mesh, in_specs=placed, out_specs=P(("bl", "freq"), None, None), check_vma=False
    )
```

profile of v0, /device:TPU:0, one launch (start us, length us, event | category | flops | bytes accessed | tf_op | source)
XLA Modules:
  0.0 386.1 jit_solution(9053859770540490229)
XLA Ops:
  6.5 0.0 copy-start.2
  6.5 0.0 reduce-scatter.2.cloned.1.call-start
  6.5 7.4 %copy.12 = bf16[256,64,64,1]{2,1,3,0:T(8,128)(2,1)} copy(bf16[256,64,64,1]{0,2,1,3:T(8,128)(2,1)} %bitcast.37) | data formatting | bytes 4194304 | tf_op args[2]
  14.0 0.0 copy-done.2
  14.0 4.6 %negate_convert_fusion = (bf16[1024,256]{0,1:T(8,128)(2,1)S(1)}, bf16[1024,256]{0,1:T(8,128)(2,1)S(1)}, bf16[1024,256]{0,1:T(8,128)(2,1)S(1)}) fusion(s32[1024]{0:T(1024)S(1)} %iota_add_fusion, s32[256]{0:T(256)S(1)} %copy-done.2), kind=kLoop, calls=%fused_computation.19 | loop fusion | flops 5242880 | bytes 1577984 | tf_op jit(solution)/shard_map/convert.7
  18.5 0.3 maximum_bitcast_fusion
  18.8 0.0 copy-start
  18.8 24.1 %fusion.2 = f32[512,64,128,1]{2,0,1,3:T(8,128)} fusion(bf16[2,64,128,1024]{3,2,1,0:T(8,128)(2,1)} %param.5, bf16[1,1024,512]{1,2,0:T(8,128)(2,1)S(1)} %get-tuple-element.6, bf16[1,1024,512]{1,2,0:T(8,128)(2,1)S(1)} %get-tuple-element.5), kind=kOutput, calls=%fused_computation.4 | convolution fusion | flops 17184063488 | bytes 52428800 | tf_op jit(solution)/shard_map/dot_general | solution.py:20
  42.9 0.0 copy-done
  42.9 26.9 %fusion = f32[256,128,2,64]{1,3,2,0:T(8,128)} fusion(bf16[256,64,64,1]{2,1,3,0:T(8,128)(2,1)S(1)} %copy-done, f32[64,128,2,256]{1,3,2,0:T(8,128)} %bitcast.34), kind=kOutput, calls=%fused_computation | convolution fusion | flops 3221225472 | bytes 35651584 | tf_op jit(solution)/shard_map/bfcm,msb->mfcs/dot_general | solution.py:29
  69.8 0.0 reduce-scatter.2.cloned.1.call-update
  69.8 156.7 %reduce-scatter.2.cloned.1.call-done = f32[64,128,128]{1,2,0:T(8,128)} async-done(((f32[256,128,128]{1,2,0:T(8,128)}), f32[64,128,128]{1,2,0:T(8,128)}) %reduce-scatter.2.cloned.1.call-update) | async-done | bytes 4194320 | tf_op jit(solution)/shard_map/reduce_scatter | solution.py:47
  226.5 98.6 %all_to_all.18 = f32[64,128,128]{1,2,0:T(8,128)S(1)} all-to-all(f32[64,128,128]{1,2,0:T(8,128)} %reduce-scatter.2.cloned.1.call-done), channel_id=1, replica_groups=mesh['bl'=4,'freq'=8] {'freq'}, dimensions={0} | all-to-all | bytes 8388608 | tf_op jit(solution)/shard_map/all_to_all | solution.py:48
  325.1 4.4 %copy.18 = f32[8,8,128,128]{2,0,3,1:T(8,128)} copy(f32[8,8,128,128]{2,3,1,0:T(8,128)S(1)} %bitcast.35) | data formatting | bytes 8388608 | tf_op jit(solution)/shard_map/all_to_all | solution.py:48
  329.5 0.0 copy-start.1
  329.5 4.9 %all_to_all.16 = f32[8,1024,128]{1,2,0:T(8,128)} reshape(f32[8,8,128,128]{2,1,3,0:T(8,128)} %bitcast.36) | data formatting | bytes 8388608 | tf_op jit(solution)/shard_map/all_to_all | solution.py:48
  334.4 0.0 copy-done.1
  334.4 39.6 %bitcast_subtract_fusion = f32[8,1024,128]{1,2,0:T(8,128)} fusion(f32[8,1024,128]{1,2,0:T(8,128)} %all_to_all.16, f32[8,1024,1024]{2,1,0:T(8,128)} %param.8, f32[8,1024]{1,0:T(8,128)S(1)} %copy-done.1), kind=kOutput, calls=%fused_computation.2 | convolution fusion | flops 12886999040 | bytes 41975808 | tf_op jit(solution)/shard_map/mfg,mgk->mfk/dot_general | solution.py:36
  374.0 5.3 %copy.10 = f32[8,1024,128]{2,1,0:T(8,128)} copy(f32[8,1024,128]{1,2,0:T(8,128)} %bitcast_subtract_fusion) | data formatting | bytes 8388608 | tf_op jit(solution)/shard_map/sub | solution.py:37
  (1 shorter events, 0.0 us)
Async XLA Ops:
  6.5 7.4 %copy-start.2 = (s32[256]{0:T(256)S(1)}, s32[256]{0:T(256)}, u32[]{:S(2)}) copy-start(s32[256]{0:T(256)} %param.6) | copy-start | bytes 3076
  6.5 220.0 %reduce-scatter.2.cloned.1.call-start = ((), (), s32[]{:S(2)}) async-start(), calls=%async_computation.2 | async-start | bytes 20971520 | tf_op jit(solution)/shard_map/reduce_scatter | solution.py:47
  18.8 24.1 %copy-start = (bf16[256,64,64,1]{2,1,3,0:T(8,128)(2,1)S(1)}, bf16[256,64,64,1]{2,1,3,0:T(8,128)(2,1)}, u32[]{:S(2)}) copy-start(bf16[256,64,64,1]{2,1,3,0:T(8,128)(2,1)} %copy.12) | copy-start | bytes 6291460
  329.5 4.9 %copy-start.1 = (f32[8,1024]{1,0:T(8,128)S(1)}, f32[8,1024]{1,0:T(8,128)}, u32[]{:S(2)}) copy-start(f32[8,1024]{1,0:T(8,128)} %param.9) | copy-start | bytes 98308
Sparse Core Ops, SparseCore 0:
  69.9 156.5 reduce-scatter.1
where the time goes:
time: 387 us; the launch traced here: 386 us
  waiting for transfers between devices  157 us (41%)
  blocking collectives  98.6 us (25%)
  matrix products  90.5 us (23%)
  local copies, waits for them, and re-layouts  22 us (6%)
  between operations  13.4 us (3%)
  other arithmetic  4.84 us (1%)
    reduce_scatter x1, waiting for transfers between devices, body(): lax.psum_scatter(partial_terms, 'bl', scatter_dimension=0, tiled=True)  157 us
    all_to_all x1, blocking collectives, body(): lax.all_to_all(summed_modes, 'freq', split_axis=0, concat_axis=1, tiled=T...  98.6 us
    dot_general x1, matrix products, weigh_all(): jnp.einsum('mfg,mgk->mfk', inverse_cov, owner_modes, precision=lax.Precis...  39.6 us
    dot_general x1, matrix products, project(): jnp.einsum('bfcm,msb->mfcs', halves, beam_rows.astype(jnp.float32), preci...  26.9 us
    dot_general x1, matrix products, transform(): lax.dot_general(samples, dft_weights, (((0, 3), (0, 1)), ((), ())), prefe...  24.1 us
    all_to_all x2, local copies, waits for them, and re-layouts, body(): lax.all_to_all(summed_modes, 'freq', split_axis=0, concat_axis=1, tiled=T...  9.26 us
  transfers between devices with their start and end apart: 1, of which 1 were waited for; matrix products, arithmetic and copies ran while one was open for 0% of the time, Pallas kernels for 0%

commit v1 on v0

--- a/solution.py
+++ b/solution.py
@@ -45,7 +45,12 @@
     dft_weights = dft_table(mode_index, sample_ids, total_times)
     partial_terms = project(transform(visibility, dft_weights), beam_mode_weights)
     summed_modes = lax.psum_scatter(partial_terms, "bl", scatter_dimension=0, tiled=True)
-    owner_modes = lax.all_to_all(summed_modes, "freq", split_axis=0, concat_axis=1, tiled=True)
+    owner_modes = jnp.concatenate(
+        jax.lax.all_to_all(
+            jnp.stack(jnp.split(summed_modes, jax.lax.axis_size("freq"), 0), 0), "freq", 0, 0
+        ),
+        1,
+    )
     return weigh_all(inverse_cov, noise_power, owner_modes)
 
 

time: 387 us -> 387 us (level)
    all_to_all x2 -> x0, local copies, waits for them, and re-layouts: 9.26 us -> none  [body(): lax.all_to_all(summed_modes, 'freq', split_axis=0, concat_axis=1, tiled=T...]
    unnamed x7 -> x14, local copies, waits for them, and re-layouts: 7.42 us -> 15 us
where the time goes in v1:
time: 387 us; the launch traced here: 386 us
  waiting for transfers between devices  157 us (41%)
  blocking collectives  98.4 us (25%)
  matrix products  91.6 us (24%)
  local copies, waits for them, and re-layouts  21.4 us (6%)
  between operations  13.5 us (3%)
  other arithmetic  4.84 us (1%)
    reduce_scatter x1, waiting for transfers between devices, body(): lax.psum_scatter(partial_terms, 'bl', scatter_dimension=0, tiled=True)  157 us
    all_to_all x1, blocking collectives, body(): jax.lax.all_to_all(jnp.stack(jnp.split(summed_modes, jax.lax.axis_size('f...  98.4 us
    dot_general x1, matrix products, weigh_all(): jnp.einsum('mfg,mgk->mfk', inverse_cov, owner_modes, precision=lax.Precis...  40.6 us
    dot_general x1, matrix products, project(): jnp.einsum('bfcm,msb->mfcs', halves, beam_rows.astype(jnp.float32), preci...  26.9 us
    dot_general x1, matrix products, transform(): lax.dot_general(samples, dft_weights, (((0, 3), (0, 1)), ((), ())), prefe...  24.1 us
    unnamed x14, local copies, waits for them, and re-layouts  15 us
  transfers between devices with their start and end apart: 1, of which 1 were waited for; matrix products, arithmetic and copies ran while one was open for 0% of the time, Pallas kernels for 0%

profile of v1, /device:TPU:0, one launch (start us, length us, event | category | flops | bytes accessed | tf_op | source)
XLA Modules:
  0.0 386.4 jit_solution(14885053515185907904)
XLA Ops:
  6.5 0.0 copy-start.2
  6.5 0.0 reduce-scatter.2.cloned.1.call-start
  6.5 7.4 %copy.12 = bf16[256,64,64,1]{2,1,3,0:T(8,128)(2,1)} copy(bf16[256,64,64,1]{0,2,1,3:T(8,128)(2,1)} %bitcast.70) | data formatting | bytes 4194304 | tf_op args[2]
  14.0 0.0 copy-done.2
  14.0 4.6 %negate_convert_fusion = (bf16[1024,256]{0,1:T(8,128)(2,1)S(1)}, bf16[1024,256]{0,1:T(8,128)(2,1)S(1)}, bf16[1024,256]{0,1:T(8,128)(2,1)S(1)}) fusion(s32[1024]{0:T(1024)S(1)} %iota_add_fusion, s32[256]{0:T(256)S(1)} %copy-done.2), kind=kLoop, calls=%fused_computation.21 | loop fusion | flops 5242880 | bytes 1577984 | tf_op jit(solution)/shard_map/convert.7
  18.5 0.3 maximum_bitcast_fusion
  18.8 0.0 copy-start
  18.8 24.1 %fusion.7 = f32[512,64,128,1]{2,0,1,3:T(8,128)} fusion(bf16[2,64,128,1024]{3,2,1,0:T(8,128)(2,1)} %param.5, bf16[1,1024,512]{1,2,0:T(8,128)(2,1)S(1)} %get-tuple-element.6, bf16[1,1024,512]{1,2,0:T(8,128)(2,1)S(1)} %get-tuple-element.5), kind=kOutput, calls=%fused_computation.6 | convolution fusion | flops 17184063488 | bytes 52428800 | tf_op jit(solution)/shard_map/dot_general | solution.py:20
  42.9 0.0 copy-done
  42.9 26.9 %fusion = f32[256,128,2,64]{1,3,2,0:T(8,128)} fusion(bf16[256,64,64,1]{2,1,3,0:T(8,128)(2,1)S(1)} %copy-done, f32[64,128,2,256]{1,3,2,0:T(8,128)} %bitcast.69), kind=kOutput, calls=%fused_computation | convolution fusion | flops 3221225472 | bytes 35651584 | tf_op jit(solution)/shard_map/bfcm,msb->mfcs/dot_general | solution.py:29
  69.8 0.0 reduce-scatter.2.cloned.1.call-update
  69.8 156.7 %reduce-scatter.2.cloned.1.call-done = f32[64,128,128]{1,2,0:T(8,128)} async-done(((f32[256,128,128]{1,2,0:T(8,128)}), f32[64,128,128]{1,2,0:T(8,128)}) %reduce-scatter.2.cloned.1.call-update) | async-done | bytes 4194320 | tf_op jit(solution)/shard_map/reduce_scatter | solution.py:47
  226.5 1.1 fusion.23
  227.6 1.1 fusion.22
  228.7 1.1 fusion.21
  229.8 1.1 fusion.20
  230.8 1.1 fusion.19
  231.9 1.1 fusion.18
  233.0 1.1 fusion.17
  234.1 1.1 fusion.16
  235.2 0.0 copy-start.1
  235.2 98.4 %all_to_all.5 = f32[8,8,128,128]{2,3,1,0:T(8,128)S(1)} all-to-all(f32[8,8,128,128]{2,3,1,0:T(8,128)S(1)} %fusion.16), channel_id=1, replica_groups=mesh['bl'=4,'freq'=8] {'freq'}, dimensions={0} | all-to-all | bytes 8388608 | tf_op jit(solution)/shard_map/all_to_all | solution.py:49
  333.6 0.0 copy-done.1
  333.6 40.6 %bitcast_subtract_fusion = f32[8,1024,128]{1,2,0:T(8,128)} fusion(f32[8,1024,1024]{2,1,0:T(8,128)} %param.8, f32[8,1024]{1,0:T(8,128)S(1)} %copy-done.1, f32[8,8,128,128]{2,3,1,0:T(8,128)S(1)} %all_to_all.5), kind=kOutput, calls=%fused_computation.2 | convolution fusion | flops 12886999040 | bytes 41975808 | tf_op jit(solution)/shard_map/mfg,mgk->mfk/dot_general | solution.py:36
  374.2 5.3 %copy.10 = f32[8,1024,128]{2,1,0:T(8,128)} copy(f32[8,1024,128]{1,2,0:T(8,128)} %bitcast_subtract_fusion) | data formatting | bytes 8388608 | tf_op jit(solution)/shard_map/sub | solution.py:37
  (1 shorter events, 0.0 us)
Async XLA Ops:
  6.5 7.4 %copy-start.2 = (s32[256]{0:T(256)S(1)}, s32[256]{0:T(256)}, u32[]{:S(2)}) copy-start(s32[256]{0:T(256)} %param.6) | copy-start | bytes 3076
  6.5 220.0 %reduce-scatter.2.cloned.1.call-start = ((), (), s32[]{:S(2)}) async-start(), calls=%async_computation.2 | async-start | bytes 20971520 | tf_op jit(solution)/shard_map/reduce_scatter | solution.py:47
  18.8 24.1 %copy-start = (bf16[256,64,64,1]{2,1,3,0:T(8,128)(2,1)S(1)}, bf16[256,64,64,1]{2,1,3,0:T(8,128)(2,1)}, u32[]{:S(2)}) copy-start(bf16[256,64,64,1]{2,1,3,0:T(8,128)(2,1)} %copy.12) | copy-start | bytes 6291460
  235.2 98.4 %copy-start.1 = (f32[8,1024]{1,0:T(8,128)S(1)}, f32[8,1024]{1,0:T(8,128)}, u32[]{:S(2)}) copy-start(f32[8,1024]{1,0:T(8,128)} %param.9) | copy-start | bytes 98308
Sparse Core Ops, SparseCore 0:
  69.9 156.5 reduce-scatter.1
